TPU v7x, 512 devices: a whole 4x4x16 slice. The times are simulated.
512 devices in a mesh: req: 32 (over y, x, core), mlp: 16 (over z).
Axes of the slice: x: 4, y: 4, z: 16, core: 2. Of those that a mesh axis runs over, the one named last changes fastest.
Arguments:
- queries: bfloat16 [12288, 4096], P('req', 'mlp')
- new_keys: bfloat16 [12288, 1024], P(('req', 'mlp')), may hold values from -5 to 5
- new_values: bfloat16 [12288, 1024], P(('req', 'mlp')), may hold values from -6 to 6
- cache_keys: bfloat16 [32, 4096, 1024], P('req', 'mlp')
- cache_values: bfloat16 [32, 4096, 1024], P('req', 'mlp'), may hold values from -6 to 6
- cache_len: int32 [32], P('req'), may hold values from 256 to 4096, as said below
- residual: bfloat16 [12288, 2560], P('req')
- out_weight: bfloat16 [4096, 2560], P('mlp'), may hold values from -0.1796875 to 0.1796875
- norm_gain: bfloat16 [2560], replicated, may hold values from 0.099609375 to 1.8984375
- gate_weight: bfloat16 [2560, 9728], P('req', 'mlp'), may hold values from -0.125 to 0.125
- up_weight: bfloat16 [2560, 9728], P('req', 'mlp'), may hold values from -0.125 to 0.125
- down_weight: bfloat16 [2560, 9728], P('req', 'mlp'), may hold values from -0.0625 to 0.0625
Outputs:
- layer_out: bfloat16 [12288, 2560], P(('req', 'mlp'))
Inputs may be any that keep to these rules, and one draw needn't show every extreme that they name: cache_len[r] counts request r's valid cached positions from the first; some request has exactly 4096.
All inputs are finite; a program needn't handle non-finite values.
Results may differ from a plain program's by a relative error of at most 0.012.
Values may be sent and summed in bfloat16 or wider, within the bound.
No kernel may reach another device: no remote copies, remote signals or barrier semaphores. Data moves between devices by JAX's collectives and lax.ppermute only.
A program may use at most 64 MiB of HBM per device.

v0:
```python
import jax
import jax.numpy as jnp
from jax import lax
from jax.sharding import PartitionSpec as P

H = 32
KVH = 8
HD = 128
norm_eps = 1e-06


def shards(
    queries,
    new_keys,
    new_values,
    cache_keys,
    cache_values,
    cache_len,
    residual,
    out_weight,
    norm_gain,
    gate_weight,
    up_weight,
    down_weight,
):
    n_mlp = lax.axis_size("mlp")
    heads_dev = H // n_mlp
    group_size = H // KVH
    kv_dev = max(1, heads_dev // group_size)
    per_kv = heads_dev // kv_dev
    query_rows = queries.shape[0]
    rows_dev = new_keys.shape[0]
    cache_total = cache_keys.shape[1] * n_mlp

    def to_slots(rows_block):
        row_count = rows_block.shape[0]
        copies = n_mlp // KVH
        spread = jnp.broadcast_to(
            rows_block.reshape(row_count, KVH, 1, HD), (row_count, KVH, copies, HD)
        )
        return spread.reshape(row_count, n_mlp, HD)

    arrived = (
        lax.all_to_all(to_slots(cache_keys[0]), "mlp", split_axis=1, concat_axis=0, tiled=True),
        lax.all_to_all(to_slots(cache_values[0]), "mlp", split_axis=1, concat_axis=0, tiled=True),
        lax.all_to_all(to_slots(new_keys), "mlp", split_axis=1, concat_axis=0, tiled=True),
        lax.all_to_all(to_slots(new_values), "mlp", split_axis=1, concat_axis=0, tiled=True),
    )
    keys_old = arrived[0]
    values_old = arrived[1]
    keys_new = arrived[2]
    values_new = arrived[3]
    grouped = queries.reshape(query_rows, kv_dev, per_kv, HD)
    score_scale = HD ** (-0.5)

    def absorb(running, key_part, value_part, allowed):
        row_max, row_sum, weighted = running
        scores = (
            jnp.einsum("tgqd,kgd->gqtk", grouped, key_part, preferred_element_type=jnp.float32)
            * score_scale
        )
        scores = jnp.where(allowed, scores, -jnp.inf)
        new_max = jnp.maximum(row_max, jnp.max(scores, axis=-1))
        shrink = jnp.exp(row_max - new_max)
        weights = jnp.exp(scores - new_max[..., None])
        row_sum = row_sum * shrink + jnp.sum(weights, axis=-1)
        weighted = weighted * shrink[..., None] + jnp.einsum(
            "gqtk,kgd->gqtd",
            weights.astype(jnp.bfloat16),
            value_part,
            preferred_element_type=jnp.float32,
        )
        return (new_max, row_sum, weighted)

    start_state = (
        jnp.full((kv_dev, per_kv, query_rows), -jnp.inf, jnp.float32),
        jnp.zeros((kv_dev, per_kv, query_rows), jnp.float32),
        jnp.zeros((kv_dev, per_kv, query_rows, HD), jnp.float32),
    )
    token_ids = lax.iota(jnp.int32, query_rows)
    causal = token_ids[None, :] <= token_ids[:, None]
    running = absorb(start_state, keys_new, values_new, causal)
    length = cache_len[0]
    key_block = min(512, cache_total)

    def visit(turn_index, running):
        offset = turn_index * key_block
        key_part = lax.dynamic_slice_in_dim(keys_old, offset, key_block, 0)
        value_part = lax.dynamic_slice_in_dim(values_old, offset, key_block, 0)
        positions = offset + lax.iota(jnp.int32, key_block)
        return absorb(running, key_part, value_part, (positions < length)[None, :])

    block_count = cache_total // key_block
    row_max, row_sum, weighted = lax.fori_loop(0, block_count, visit, running)
    attended = (weighted / row_sum[..., None]).astype(jnp.bfloat16)
    attended = attended.transpose(2, 0, 1, 3).reshape(query_rows, heads_dev * HD)
    partial_value = jnp.dot(attended, out_weight, preferred_element_type=jnp.float32)
    row_start = lax.axis_index("mlp") * rows_dev
    head_sum = lax.psum(partial_value.astype(jnp.bfloat16), "mlp").astype(jnp.float32)
    stream = (residual.astype(jnp.float32) + head_sum).astype(jnp.bfloat16)
    stream_full = stream.astype(jnp.float32)
    factor = lax.rsqrt(jnp.mean(stream_full * stream_full, axis=-1, keepdims=True) + norm_eps)
    normed = (stream_full * factor * norm_gain.astype(jnp.float32)).astype(jnp.bfloat16)
    stream_rows = lax.dynamic_slice_in_dim(stream, row_start, rows_dev, 0)
    gate_sum = jnp.dot(
        normed,
        lax.all_gather(gate_weight, "req", axis=0, tiled=True),
        preferred_element_type=jnp.float32,
    )
    up_sum = jnp.dot(
        normed,
        lax.all_gather(up_weight, "req", axis=0, tiled=True),
        preferred_element_type=jnp.float32,
    )
    hidden = (jax.nn.silu(gate_sum) * up_sum).astype(jnp.bfloat16)
    mlp_part = lax.dot_general(
        hidden,
        lax.all_gather(down_weight, "req", axis=0, tiled=True),
        (((1,), (1,)), ((), ())),
        preferred_element_type=jnp.float32,
    )
    mlp_rows = lax.psum_scatter(
        mlp_part.astype(jnp.bfloat16), "mlp", scatter_dimension=0, tiled=True
    ).astype(jnp.float32)
    return (stream_rows.astype(jnp.float32) + mlp_rows).astype(jnp.bfloat16)


def solution(mesh):
    in_specs = (
        P("req", "mlp"),
        P(("req", "mlp"), None),
        P(("req", "mlp"), None),
        P("req", "mlp", None),
        P("req", "mlp", None),
        P("req"),
        P("req", None),
        P("mlp", None),
        P(),
        P("req", "mlp"),
        P("req", "mlp"),
        P("req", "mlp"),
    )
    out_specs = P(("req", "mlp"), None)
    return jax.shard_map(shards, mesh=mesh, in_specs=in_specs, out_specs=out_specs, check_vma=False)
```

profile of v0, /device:TPU:2, one launch (start us, length us, event | category | flops | bytes accessed | tf_op | source)
XLA Modules:
  0.0 472.2 jit_solution(10438826310127697672)
XLA Ops:
  7.4 0.9 copy_bitcast_fusion.1
  8.3 0.7 broadcast_in_dim.89
  8.9 15.2 %all-to-all-start = ((bf16[24,16,128]{2,0,1:T(8,128)(2,1)}), bf16[24,16,128]{2,0,1:T(8,128)(2,1)S(1)}, u32[]{:S(2)}, u32[]{:S(2)}) async-start(bf16[24,16,128]{2,0,1:T(8,128)(2,1)} %bitcast.13), calls=%async_computation | async-start | bytes 196608 | tf_op jit(solution)/shard_map/all_to_all | solution.py:46
  24.1 0.8 copy_bitcast_fusion
  25.0 12.7 %all-to-all-done = bf16[24,16,128]{2,0,1:T(8,128)(2,1)S(1)} async-done(((bf16[24,16,128]{2,0,1:T(8,128)(2,1)}), bf16[24,16,128]{2,0,1:T(8,128)(2,1)S(1)}, u32[]{:S(2)}, u32[]{:S(2)}) %all-to-all-start) | async-done | bytes 98336 | tf_op jit(solution)/shard_map/all_to_all | solution.py:46
  37.7 0.7 broadcast_in_dim.96
  38.4 3.6 all-to-all-start.1
  41.9 1.1 copy.35
  43.2 11.9 %all-to-all-done.1 = bf16[24,16,128]{2,0,1:T(8,128)(2,1)S(1)} async-done(((bf16[24,16,128]{2,0,1:T(8,128)(2,1)}), bf16[24,16,128]{2,0,1:T(8,128)(2,1)S(1)}, u32[]{:S(2)}, u32[]{:S(2)}) %all-to-all-start.1) | async-done | bytes 98336 | tf_op jit(solution)/shard_map/all_to_all | solution.py:47
  55.1 1.2 broadcast_in_dim.98
  56.3 3.7 all-to-all-start.2
  60.1 48.7 %all-to-all-done.2 = bf16[256,16,128]{2,0,1:T(8,128)(2,1)S(1)} async-done(((bf16[256,16,128]{2,0,1:T(8,128)(2,1)}), bf16[256,16,128]{2,0,1:T(8,128)(2,1)S(1)}, u32[]{:S(2)}, u32[]{:S(2)}) %all-to-all-start.2) | async-done | bytes 1048608 | tf_op jit(solution)/shard_map/all_to_all | solution.py:44
  108.9 1.3 broadcast_in_dim.100
  110.2 7.9 %all-to-all-start.3 = ((bf16[256,16,128]{2,0,1:T(8,128)(2,1)}), bf16[256,16,128]{2,0,1:T(8,128)(2,1)S(1)}, u32[]{:S(2)}, u32[]{:S(2)}) async-start(bf16[256,16,128]{2,0,1:T(8,128)(2,1)} %bitcast.35), calls=%async_computation.3 | async-start | bytes 2097152 | tf_op jit(solution)/shard_map/all_to_all | solution.py:45
  118.3 0.2 copy.28
  118.5 0.4 fusion.35
  118.9 0.2 fusion.23
  119.1 0.4 fusion.21
  119.5 48.7 %all-to-all-done.3 = bf16[256,16,128]{2,0,1:T(8,128)(2,1)S(1)} async-done(((bf16[256,16,128]{2,0,1:T(8,128)(2,1)}), bf16[256,16,128]{2,0,1:T(8,128)(2,1)S(1)}, u32[]{:S(2)}, u32[]{:S(2)}) %all-to-all-start.3) | async-done | bytes 1048608 | tf_op jit(solution)/shard_map/all_to_all | solution.py:45
  168.2 22.4 %while.17 = (s32[]{:T(128)}, f32[1,2,384]{2,1,0:T(2,128)S(1)}, f32[1,2,384]{2,1,0:T(2,128)S(1)}, f32[1,2,384,128]{3,2,1,0:T(8,128)S(1)}, s32[]{:T(128)}, /*index...) while((s32[]{:T(128)}, f32[1,2,384]{2,1,0:T(2,128)S(1)}, ...), condition=%wide.region_5.6_spmd, body=%wide.region_2.5_spmd.sunk | while | flops 204279040 | bytes 6014131 | solution.py:94
  168.2 0.7 add_compare_fusion.2
  168.8 1.3 bitcast_reduce_fusion.2
  170.2 0.5 fusion.55
  170.7 0.2 fusion.54
  171.0 0.7 add_compare_fusion.2
  171.7 1.3 bitcast_reduce_fusion.2
  173.0 0.5 fusion.55
  173.5 0.2 fusion.54
  173.8 0.7 add_compare_fusion.2
  174.5 1.3 bitcast_reduce_fusion.2
  175.8 0.5 fusion.55
  176.3 0.2 fusion.54
  176.6 0.7 add_compare_fusion.2
  177.3 1.3 bitcast_reduce_fusion.2
  178.6 0.5 fusion.55
  179.1 0.2 fusion.54
  179.4 0.7 add_compare_fusion.2
  180.1 1.3 bitcast_reduce_fusion.2
  181.4 0.5 fusion.55
  181.9 0.2 fusion.54
  182.2 0.7 add_compare_fusion.2
  182.9 1.3 bitcast_reduce_fusion.2
  184.2 0.5 fusion.55
  184.7 0.2 fusion.54
  185.0 0.7 add_compare_fusion.2
  185.7 1.3 bitcast_reduce_fusion.2
  187.0 0.5 fusion.55
  187.5 0.2 fusion.54
  187.8 0.7 add_compare_fusion.2
  188.5 1.3 bitcast_reduce_fusion.2
  189.8 0.5 fusion.55
  190.4 0.2 fusion.54
  190.6 0.2 copy.29
  190.8 2.1 convolution_convert_fusion.1
  193.0 0.5 all-gather.4.cloned.1.call-update
  193.6 0.5 all-gather.6.cloned.1.call-update
  194.2 0.5 all-gather.8.cloned.1.call-update
  194.8 139.0 %all-reduce.2.cloned.1.call-done = bf16[384,2560]{1,0:T(8,128)(2,1)} async-done(((bf16[384,2560]{1,0:T(8,128)(2,1)}), bf16[384,2560]{1,0:T(8,128)(2,1)}) %all-reduce.2.cloned.1.call-update) | async-done | bytes 1966096 | tf_op jit(solution)/shard_map/psum | solution.py:99
  333.8 3.0 fusion.15
  336.8 4.8 %fusion.29 = f32[384,608]{0,1:T(8,128)} fusion(bf16[2560,608]{1,0:T(8,128)(2,1)} %all-gather.4.cloned.1.call-done, bf16[384,2560]{1,0:T(8,128)(2,1)S(1)} %get-tuple-element.174, f32[2560]{0:T(1024)S(1)} %convert_element_type.57, f32[384]{0:T(512)S(1)} %add_rsqrt_fusion), kind=kOutput, calls=%fused_computation.43 | convolution fusion | flops 1199308800 | bytes 6024704 | tf_op jit(solution)/shard_map/dot_general | solution.py:105
  341.6 40.2 %all-gather.8.cloned.1.call-done = bf16[2560,608]{1,0:T(8,128)(2,1)} async-done(((bf16[80,608]{1,0:T(8,128)(2,1)}), bf16[2560,608]{1,0:T(8,128)(2,1)}) %all-gather.8.cloned.1.call-update) | async-done | bytes 3112976 | tf_op jit(solution)/shard_map/all_gather | solution.py:118
  381.8 8.1 %convolution_convert_fusion = bf16[384,2560]{1,0:T(8,128)(2,1)} fusion(bf16[2560,608]{1,0:T(8,128)(2,1)} %all-gather.8.cloned.1.call-done, bf16[2560,608]{1,0:T(8,128)(2,1)} %all-gather.6.cloned.1.call-done, f32[384,608]{0,1:T(8,128)} %fusion.29, bf16[384,2560]{1,0:T(8,128)(2,1)S(1)} %get-tuple-element.174, f32[2560]{0:T(1024)S(1)} %convert_element_type.57, ...), kind=kOutput, calls=%fused_computation.24 | convolution fusion | flops 2397069312 | bytes 11103744 | tf_op jit(solution)/shard_map/dot_general | solution.py:116
  389.9 73.1 %reduce-scatter.2.cloned.1.call-done = bf16[24,2560]{1,0:T(8,128)(2,1)} async-done(((bf16[384,2560]{1,0:T(8,128)(2,1)}), bf16[24,2560]{1,0:T(8,128)(2,1)}) %reduce-scatter.2.cloned.1.call-update) | async-done | bytes 122896 | tf_op jit(solution)/shard_map/reduce_scatter | solution.py:122
  463.0 1.6 add_convert_fusion.1
  (53 shorter events, 1.0 us)
Async XLA Ops:
  7.4 183.5 %copy-start = (bf16[256,2560]{1,0:T(8,128)(2,1)S(1)}, bf16[256,2560]{1,0:T(8,128)(2,1)}, u32[]{:S(2)}) copy-start(bf16[256,2560]{1,0:T(8,128)(2,1)} %param.21) | copy-start | bytes 3932164
  8.9 28.8 %all-to-all-start = ((bf16[24,16,128]{2,0,1:T(8,128)(2,1)}), bf16[24,16,128]{2,0,1:T(8,128)(2,1)S(1)}, u32[]{:S(2)}, u32[]{:S(2)}) async-start(bf16[24,16,128]{2,0,1:T(8,128)(2,1)} %bitcast.13), calls=%async_computation | async-start | bytes 196608 | tf_op jit(solution)/shard_map/all_to_all | solution.py:46
  38.4 16.8 %all-to-all-start.1 = ((bf16[24,16,128]{2,0,1:T(8,128)(2,1)}), bf16[24,16,128]{2,0,1:T(8,128)(2,1)S(1)}, u32[]{:S(2)}, u32[]{:S(2)}) async-start(bf16[24,16,128]{2,0,1:T(8,128)(2,1)} %bitcast.23), calls=%async_computation.1 | async-start | bytes 196608 | tf_op jit(solution)/shard_map/all_to_all | solution.py:47
  43.2 16.8 %copy-start.2 = (bf16[1,256,1024]{2,1,0:T(8,128)(2,1)S(1)}, bf16[1,256,1024]{2,1,0:T(8,128)(2,1)}, u32[]{:S(2)}) copy-start(bf16[1,256,1024]{2,1,0:T(8,128)(2,1)} %param.18) | copy-start | bytes 1572868
  56.3 52.6 %all-to-all-start.2 = ((bf16[256,16,128]{2,0,1:T(8,128)(2,1)}), bf16[256,16,128]{2,0,1:T(8,128)(2,1)S(1)}, u32[]{:S(2)}, u32[]{:S(2)}) async-start(bf16[256,16,128]{2,0,1:T(8,128)(2,1)} %bitcast.30), calls=%async_computation.2 | async-start | bytes 2097152 | tf_op jit(solution)/shard_map/all_to_all | solution.py:44
  60.1 58.0 %copy-start.3 = (bf16[384,256]{1,0:T(8,128)(2,1)S(1)}, bf16[384,256]{1,0:T(8,128)(2,1)}, u32[]{:S(2)}) copy-start(bf16[384,256]{1,0:T(8,128)(2,1)} %param.14) | copy-start | bytes 589828
  108.8 1.3 copy-start.1
  110.2 58.0 %all-to-all-start.3 = ((bf16[256,16,128]{2,0,1:T(8,128)(2,1)}), bf16[256,16,128]{2,0,1:T(8,128)(2,1)S(1)}, u32[]{:S(2)}, u32[]{:S(2)}) async-start(bf16[256,16,128]{2,0,1:T(8,128)(2,1)} %bitcast.35), calls=%async_computation.3 | async-start | bytes 2097152 | tf_op jit(solution)/shard_map/all_to_all | solution.py:45
  118.1 215.7 %all-reduce.2.cloned.1.call-start = ((), (), s32[]{:S(2)}) async-start(), calls=%async_computation.5 | async-start | bytes 3932160 | tf_op jit(solution)/shard_map/psum | solution.py:99
  192.9 1.8 copy-start.4
  193.0 143.8 %all-gather.4.cloned.1.call-start = ((), (), s32[]{:S(2)}) async-start(), calls=%async_computation.6 | async-start | bytes 3379200 | tf_op jit(solution)/shard_map/all_gather | solution.py:107
  193.5 148.1 %all-gather.6.cloned.1.call-start = ((), (), s32[]{:S(2)}) async-start(), calls=%async_computation.7 | async-start | bytes 3379200 | tf_op jit(solution)/shard_map/all_gather | solution.py:112
  194.1 187.7 %all-gather.8.cloned.1.call-start = ((), (), s32[]{:S(2)}) async-start(), calls=%async_computation.8 | async-start | bytes 3379200 | tf_op jit(solution)/shard_map/all_gather | solution.py:118
  194.7 268.3 %reduce-scatter.2.cloned.1.call-start = ((), (), s32[]{:S(2)}) async-start(), calls=%async_computation.9 | async-start | bytes 2088960 | tf_op jit(solution)/shard_map/reduce_scatter | solution.py:122
Sparse Core Ops, SparseCore 0:
  193.1 140.6 all-reduce.1
  390.1 72.9 reduce-scatter.1
Sparse Core Ops, SparseCore 1:
  197.1 57.5 all-gather.3
  258.3 59.9 all-gather.5
  321.8 59.9 all-gather.7
where the time goes:
time: 473 us; the launch traced here: 472 us
  waiting for transfers between devices  376 us (79%)
  starting transfers between devices  30.5 us (6%)
  matrix products  30.4 us (6%)
  between operations  15.2 us (3%)
  other arithmetic  12.1 us (3%)
  local copies, waits for them, and re-layouts  7.44 us (2%)
    psum x1, waiting for transfers between devices, shards(): lax.psum(partial_value.astype(jnp.bfloat16), 'mlp').astype(jnp.float32)  139 us
    reduce_scatter x1, waiting for transfers between devices, shards(): lax.psum_scatter(mlp_part.astype(jnp.bfloat16), 'mlp', scatter_dimension=...  73.1 us
    all_to_all x1, waiting for transfers between devices, shards(): lax.all_to_all(to_slots(cache_keys[0]), 'mlp', split_axis=1, concat_axis=...  48.7 us
    all_to_all x1, waiting for transfers between devices, shards(): lax.all_to_all(to_slots(cache_values[0]), 'mlp', split_axis=1, concat_axi...  48.7 us
    all_gather x1, waiting for transfers between devices, shards(): lax.all_gather(down_weight, 'req', axis=0, tiled=True)  40.2 us
    all_to_all x1, starting transfers between devices, shards(): lax.all_to_all(to_slots(new_keys), 'mlp', split_axis=1, concat_axis=0, ti...  15.2 us
    all_to_all x1, waiting for transfers between devices, shards(): lax.all_to_all(to_slots(new_keys), 'mlp', split_axis=1, concat_axis=0, ti...  12.7 us
    all_to_all x1, waiting for transfers between devices, shards(): lax.all_to_all(to_slots(new_values), 'mlp', split_axis=1, concat_axis=0,...  11.9 us
  transfers between devices with their start and end apart: 9, of which 7 were waited for; matrix products, arithmetic and copies ran while one was open for 2% of the time, Pallas kernels for 0%

commit v1 on v0

--- a/solution.py
+++ b/solution.py
@@ -7,6 +7,22 @@
 KVH = 8
 HD = 128
 norm_eps = 1e-06
+
+
+def pairwise_exchange(array, axis, split, join):
+    ways, here = (lax.axis_size(axis), lax.axis_index(axis))
+    width = array.shape[split] // ways
+    shape = list(array.shape)
+    shape[split] = width
+    height = shape[join]
+    shape[join] = height * ways
+    full = jnp.zeros(shape, array.dtype)
+    for mask in range(ways):
+        part = lax.dynamic_slice_in_dim(array, (here ^ mask) * width, width, axis=split)
+        if mask:
+            part = lax.ppermute(part, axis, [(d, d ^ mask) for d in range(ways)])
+        full = lax.dynamic_update_slice_in_dim(full, part, (here ^ mask) * height, axis=join)
+    return full
 
 
 def shards(
@@ -44,7 +60,7 @@
         lax.all_to_all(to_slots(cache_keys[0]), "mlp", split_axis=1, concat_axis=0, tiled=True),
         lax.all_to_all(to_slots(cache_values[0]), "mlp", split_axis=1, concat_axis=0, tiled=True),
         lax.all_to_all(to_slots(new_keys), "mlp", split_axis=1, concat_axis=0, tiled=True),
-        lax.all_to_all(to_slots(new_values), "mlp", split_axis=1, concat_axis=0, tiled=True),
+        pairwise_exchange(to_slots(new_values), "mlp", 1, 0),
     )
     keys_old = arrived[0]
     values_old = arrived[1]

time: 473 us -> 494 us (1.044)
  starting transfers between devices: 30.5 us -> 113 us
  waiting for transfers between devices: 376 us -> 307 us
    ppermute x0 -> x15, starting transfers between devices: none -> 90.4 us  [pairwise_exchange(): part = lax.ppermute(part, axis, [(d, d ^ mask) for d in range(ways)])]
    all_to_all x1, waiting for transfers between devices: 48.7 us -> 0.01 us  [shards(): lax.all_to_all(to_slots(cache_keys[0]), 'mlp', split_axis=1, concat_axis=...]
    all_to_all x1, waiting for transfers between devices: 48.7 us -> 0.01 us  [shards(): lax.all_to_all(to_slots(cache_values[0]), 'mlp', split_axis=1, concat_axi...]
    ppermute x0 -> x15, waiting for transfers between devices: none -> 39 us  [pairwise_exchange(): part = lax.ppermute(part, axis, [(d, d ^ mask) for d in range(ways)])]
    all_to_all x1 -> x0, waiting for transfers between devices: 11.9 us -> none  [shards(): lax.all_to_all(to_slots(new_values), 'mlp', split_axis=1, concat_axis=0,...]
  transfers between devices with their start and end apart: 9 -> 23, of which waited for: 7 -> 7; matrix products, arithmetic and copies ran while one was open for 2% -> 4% of each run, Pallas kernels for 0% -> 0%
where the time goes in v1:
time: 494 us; the launch traced here: 493 us
  waiting for transfers between devices  307 us (62%)
  starting transfers between devices  113 us (23%)
  matrix products  31.3 us (6%)
  between operations  15.8 us (3%)
  other arithmetic  12.8 us (3%)
  local copies, waits for them, and re-layouts  12.1 us (2%)
    psum x1, waiting for transfers between devices, shards(): lax.psum(partial_value.astype(jnp.bfloat16), 'mlp').astype(jnp.float32)  141 us
    ppermute x15, starting transfers between devices, pairwise_exchange(): part = lax.ppermute(part, axis, [(d, d ^ mask) for d in range(ways)])  90.4 us
    reduce_scatter x1, waiting for transfers between devices, shards(): lax.psum_scatter(mlp_part.astype(jnp.bfloat16), 'mlp', scatter_dimension=...  73 us
    all_gather x1, waiting for transfers between devices, shards(): lax.all_gather(down_weight, 'req', axis=0, tiled=True)  40.6 us
    ppermute x15, waiting for transfers between devices, pairwise_exchange(): part = lax.ppermute(part, axis, [(d, d ^ mask) for d in range(ways)])  39 us
    all_to_all x1, starting transfers between devices, shards(): lax.all_to_all(to_slots(new_keys), 'mlp', split_axis=1, concat_axis=0, ti...  15.2 us
    all_to_all x1, waiting for transfers between devices, shards(): lax.all_to_all(to_slots(new_keys), 'mlp', split_axis=1, concat_axis=0, ti...  12.3 us
    dot_general x9, matrix products, absorb(): jnp.einsum('tgqd,kgd->gqtk', grouped, key_part, preferred_element_type=jn...  11.6 us
  transfers between devices with their start and end apart: 23, of which 7 were waited for; matrix products, arithmetic and copies ran while one was open for 4% of the time, Pallas kernels for 0%

profile of v1, /device:TPU:2, one launch (start us, length us, event | category | flops | bytes accessed | tf_op | source)
XLA Modules:
  0.0 492.9 jit_solution(4077958662399857898)
XLA Ops:
  7.4 0.9 copy_bitcast_fusion.1
  8.3 0.7 broadcast_in_dim.90
  8.9 15.2 %all-to-all-start = ((bf16[24,16,128]{2,0,1:T(8,128)(2,1)}), bf16[24,16,128]{2,0,1:T(8,128)(2,1)S(1)}, u32[]{:S(2)}, u32[]{:S(2)}) async-start(bf16[24,16,128]{2,0,1:T(8,128)(2,1)} %bitcast.13), calls=%async_computation | async-start | bytes 196608 | tf_op jit(solution)/shard_map/all_to_all | solution.py:62
  24.1 1.1 copy.35
  25.4 12.3 %all-to-all-done = bf16[24,16,128]{2,0,1:T(8,128)(2,1)S(1)} async-done(((bf16[24,16,128]{2,0,1:T(8,128)(2,1)}), bf16[24,16,128]{2,0,1:T(8,128)(2,1)S(1)}, u32[]{:S(2)}, u32[]{:S(2)}) %all-to-all-start) | async-done | bytes 98336 | tf_op jit(solution)/shard_map/all_to_all | solution.py:62
  37.7 1.2 broadcast_in_dim.99
  38.9 3.7 all-to-all-start.1
  42.7 0.7 constant_dynamic-slice_fusion
  43.4 3.6 collective-permute-start
  47.1 4.3 collective-permute-start.1
  51.3 2.2 collective-permute-start.2
  53.5 7.6 %collective-permute-start.3 = (bf16[24,1,128]{2,0,1:T(8,128)(2,1)}, bf16[24,1,128]{2,0,1:T(8,128)(2,1)}, u32[]{:S(2)}, u32[]{:S(2)}) collective-permute-start(bf16[24,1,128]{2,0,1:T(8,128)(2,1)} %get-tuple-element.188), channel_id=1, source_target_pairs={{0,4},{1,5},{2,6},{3,7},{4,0},{5,1},{6,2},{7,3},{8,12},{9,13},{10,... | collective-permute-start | bytes 18440 | tf_op jit(solution)/shard_map/ppermute | solution.py:23
  61.1 2.5 collective-permute-start.4
  63.6 0.7 iota_compare_fusion
  64.6 1.1 copy.26
  66.0 23.3 %collective-permute-done = bf16[24,1,128]{2,0,1:T(8,128)(2,1)} collective-permute-done((bf16[24,1,128]{2,0,1:T(8,128)(2,1)}, bf16[24,1,128]{2,0,1:T(8,128)(2,1)}, u32[]{:S(2)}, u32[]{:S(2)}) %collective-permute-start) | collective-permute-done | bytes 6176 | tf_op jit(solution)/shard_map/ppermute | solution.py:23
  89.3 9.2 %collective-permute-start.5 = (bf16[24,1,128]{2,0,1:T(8,128)(2,1)}, bf16[24,1,128]{2,0,1:T(8,128)(2,1)S(1)}, u32[]{:S(2)}, u32[]{:S(2)}) collective-permute-start(bf16[24,1,128]{2,0,1:T(8,128)(2,1)} %get-tuple-element.186), channel_id=1, source_target_pairs={{0,6},{1,7},{2,4},{3,5},{4,2},{5,3},{6,0},{7,1},{8,14},{9,15},{10,... | collective-permute-start | bytes 18440 | tf_op jit(solution)/shard_map/ppermute | solution.py:23
  98.5 0.7 constant_dynamic-update-slice_fusion.14
  99.2 2.2 collective-permute-start.6
  101.4 0.7 constant_dynamic-update-slice_fusion.13
  102.1 12.6 %collective-permute-start.7 = (bf16[24,1,128]{2,0,1:T(8,128)(2,1)}, bf16[24,1,128]{2,0,1:T(8,128)(2,1)}, u32[]{:S(2)}, u32[]{:S(2)}) collective-permute-start(bf16[24,1,128]{2,0,1:T(8,128)(2,1)} %get-tuple-element.184), channel_id=1, source_target_pairs={{0,8},{1,9},{2,10},{3,11},{4,12},{5,13},{6,14},{7,15},{8,0},{9,1},... | collective-permute-start | bytes 18440 | tf_op jit(solution)/shard_map/ppermute | solution.py:23
  114.7 1.3 broadcast_in_dim.101
  116.1 3.7 all-to-all-start.2
  119.8 0.7 constant_dynamic-update-slice_fusion.12
  120.5 11.6 %collective-permute-start.8 = (bf16[24,1,128]{2,0,1:T(8,128)(2,1)S(1)}, bf16[24,1,128]{2,0,1:T(8,128)(2,1)S(1)}, u32[]{:S(2)}, u32[]{:S(2)}) collective-permute-start(bf16[24,1,128]{2,0,1:T(8,128)(2,1)S(1)} %copy-done.7), channel_id=1, source_target_pairs={{0,9},{1,8},{2,11},{3,10},{4,13},{5,12},{6,15},{7,14},{8,1},{9,0},... | collective-permute-start | bytes 18440 | tf_op jit(solution)/shard_map/ppermute | solution.py:23
  132.1 0.7 constant_dynamic-update-slice_fusion.11
  132.8 3.3 collective-permute-start.9
  136.1 0.7 constant_dynamic-update-slice_fusion.10
  136.8 9.4 %collective-permute-start.10 = (bf16[24,1,128]{2,0,1:T(8,128)(2,1)S(1)}, bf16[24,1,128]{2,0,1:T(8,128)(2,1)S(1)}, u32[]{:S(2)}, u32[]{:S(2)}) collective-permute-start(bf16[24,1,128]{2,0,1:T(8,128)(2,1)S(1)} %get-tuple-element.181), channel_id=1, source_target_pairs={{0,11},{1,10},{2,9},{3,8},{4,15},{5,14},{6,13},{7,12},{8,3},{9,2},... | collective-permute-start | bytes 18440 | tf_op jit(solution)/shard_map/ppermute | solution.py:23
  146.3 2.4 collective-permute-start.11
  148.7 7.3 %collective-permute-start.12 = (bf16[24,1,128]{2,0,1:T(8,128)(2,1)S(1)}, bf16[24,1,128]{2,0,1:T(8,128)(2,1)S(1)}, u32[]{:S(2)}, u32[]{:S(2)}) collective-permute-start(bf16[24,1,128]{2,0,1:T(8,128)(2,1)S(1)} %get-tuple-element.179), channel_id=1, source_target_pairs={{0,13},{1,12},{2,15},{3,14},{4,9},{5,8},{6,11},{7,10},{8,5},{9,4},... | collective-permute-start | bytes 18440 | tf_op jit(solution)/shard_map/ppermute | solution.py:23
  156.1 0.7 constant_dynamic-update-slice_fusion.7
  156.8 13.7 %collective-permute-done.8 = bf16[24,1,128]{2,0,1:T(8,128)(2,1)S(1)} collective-permute-done((bf16[24,1,128]{2,0,1:T(8,128)(2,1)S(1)}, bf16[24,1,128]{2,0,1:T(8,128)(2,1)S(1)}, u32[]{:S(2)}, u32[]{:S(2)}) %collective-permute-start.8) | collective-permute-done | bytes 6176 | tf_op jit(solution)/shard_map/ppermute | solution.py:23
  170.4 7.6 %collective-permute-start.13 = (bf16[24,1,128]{2,0,1:T(8,128)(2,1)S(1)}, bf16[24,1,128]{2,0,1:T(8,128)(2,1)S(1)}, u32[]{:S(2)}, u32[]{:S(2)}) collective-permute-start(bf16[24,1,128]{2,0,1:T(8,128)(2,1)S(1)} %get-tuple-element.178), channel_id=1, source_target_pairs={{0,14},{1,15},{2,12},{3,13},{4,10},{5,11},{6,8},{7,9},{8,6},{9,7},... | collective-permute-start | bytes 18440 | tf_op jit(solution)/shard_map/ppermute | solution.py:23
  178.1 4.6 collective-permute-start.14
  182.8 2.0 collective-permute-done.14
  184.9 1.3 fusion.37
  186.7 22.5 %while.17 = (s32[]{:T(128)}, f32[1,2,384]{2,1,0:T(2,128)S(1)}, f32[1,2,384]{2,1,0:T(2,128)S(1)}, f32[1,2,384,128]{3,2,1,0:T(8,128)S(1)}, s32[]{:T(128)}, /*index...) while((s32[]{:T(128)}, f32[1,2,384]{2,1,0:T(2,128)S(1)}, ...), condition=%wide.region_5.6_spmd, body=%wide.region_2.5_spmd.sunk | while | flops 204279040 | bytes 6014131 | solution.py:110
  186.8 0.7 add_compare_fusion.2
  187.4 1.3 bitcast_reduce_fusion.2
  188.7 0.6 fusion.56
  189.6 0.7 add_compare_fusion.2
  190.2 1.3 bitcast_reduce_fusion.2
  192.4 0.7 add_compare_fusion.2
  193.0 1.3 bitcast_reduce_fusion.2
  195.2 0.7 add_compare_fusion.2
  195.8 1.3 bitcast_reduce_fusion.2
  197.2 0.6 fusion.56
  198.0 0.7 add_compare_fusion.2
  198.7 1.3 bitcast_reduce_fusion.2
  200.8 0.7 add_compare_fusion.2
  201.5 1.3 bitcast_reduce_fusion.2
  203.6 0.7 add_compare_fusion.2
  204.3 1.3 bitcast_reduce_fusion.2
  206.4 0.7 add_compare_fusion.2
  207.1 1.3 bitcast_reduce_fusion.2
  209.5 2.0 convolution_convert_fusion.1
  213.5 140.7 %all-reduce.2.cloned.1.call-done = bf16[384,2560]{1,0:T(8,128)(2,1)} async-done(((bf16[384,2560]{1,0:T(8,128)(2,1)}), bf16[384,2560]{1,0:T(8,128)(2,1)}) %all-reduce.2.cloned.1.call-update) | async-done | bytes 1966096 | tf_op jit(solution)/shard_map/psum | solution.py:115
  354.2 3.0 fusion.15
  357.3 4.8 fusion.29
  362.0 40.6 %all-gather.8.cloned.1.call-done = bf16[2560,608]{1,0:T(8,128)(2,1)} async-done(((bf16[80,608]{1,0:T(8,128)(2,1)}), bf16[2560,608]{1,0:T(8,128)(2,1)}) %all-gather.8.cloned.1.call-update) | async-done | bytes 3112976 | tf_op jit(solution)/shard_map/all_gather | solution.py:134
  402.6 8.2 %convolution_convert_fusion = bf16[384,2560]{1,0:T(8,128)(2,1)} fusion(bf16[2560,608]{1,0:T(8,128)(2,1)} %all-gather.8.cloned.1.call-done, bf16[2560,608]{1,0:T(8,128)(2,1)} %all-gather.6.cloned.1.call-done, f32[384,608]{0,1:T(8,128)} %fusion.29, bf16[384,2560]{1,0:T(8,128)(2,1)S(1)} %get-tuple-element.174, f32[2560]{0:T(1024)S(1)} %convert_element_type.57, ...), kind=kOutput, calls=%fused_computation.24 | convolution fusion | flops 2397069312 | bytes 11103744 | tf_op jit(solution)/shard_map/dot_general | solution.py:132
  410.7 73.0 %reduce-scatter.2.cloned.1.call-done = bf16[24,2560]{1,0:T(8,128)(2,1)} async-done(((bf16[384,2560]{1,0:T(8,128)(2,1)}), bf16[24,2560]{1,0:T(8,128)(2,1)}) %reduce-scatter.2.cloned.1.call-update) | async-done | bytes 122896 | tf_op jit(solution)/shard_map/reduce_scatter | solution.py:138
  483.8 1.6 add_convert_fusion.1
  (107 shorter events, 8.9 us)
Async XLA Ops:
  7.4 202.1 %copy-start = (bf16[256,2560]{1,0:T(8,128)(2,1)S(1)}, bf16[256,2560]{1,0:T(8,128)(2,1)}, u32[]{:S(2)}) copy-start(bf16[256,2560]{1,0:T(8,128)(2,1)} %param.21) | copy-start | bytes 3932164
  8.9 28.8 %all-to-all-start = ((bf16[24,16,128]{2,0,1:T(8,128)(2,1)}), bf16[24,16,128]{2,0,1:T(8,128)(2,1)S(1)}, u32[]{:S(2)}, u32[]{:S(2)}) async-start(bf16[24,16,128]{2,0,1:T(8,128)(2,1)} %bitcast.13), calls=%async_computation | async-start | bytes 196608 | tf_op jit(solution)/shard_map/all_to_all | solution.py:62
  25.4 17.3 %copy-start.6 = (bf16[24,1024]{1,0:T(8,128)(2,1)S(1)}, bf16[24,1024]{1,0:T(8,128)(2,1)}, u32[]{:S(2)}) copy-start(bf16[24,1024]{1,0:T(8,128)(2,1)} %param.16) | copy-start | bytes 147460
  25.4 39.0 %copy-start.2 = (bf16[1,256,1024]{2,1,0:T(8,128)(2,1)S(1)}, bf16[1,256,1024]{2,1,0:T(8,128)(2,1)}, u32[]{:S(2)}) copy-start(bf16[1,256,1024]{2,1,0:T(8,128)(2,1)} %param.18) | copy-start | bytes 1572868
  37.7 1.2 copy-start.4
  38.9 75.8 %all-to-all-start.1 = ((bf16[256,16,128]{2,0,1:T(8,128)(2,1)}), bf16[256,16,128]{2,0,1:T(8,128)(2,1)S(1)}, u32[]{:S(2)}, u32[]{:S(2)}) async-start(bf16[256,16,128]{2,0,1:T(8,128)(2,1)} %bitcast.43), calls=%async_computation.1 | async-start | bytes 2097152 | tf_op jit(solution)/shard_map/all_to_all | solution.py:60
  43.4 45.9 %collective-permute-start = (bf16[24,1,128]{2,0,1:T(8,128)(2,1)}, bf16[24,1,128]{2,0,1:T(8,128)(2,1)}, u32[]{:S(2)}, u32[]{:S(2)}) collective-permute-start(bf16[24,1,128]{2,0,1:T(8,128)(2,1)} %get-tuple-element.191), channel_id=1, source_target_pairs={{0,1},{1,0},{2,3},{3,2},{4,5},{5,4},{6,7},{7,6},{8,9},{9,8},{10,11... | collective-permute-start | bytes 18440 | tf_op jit(solution)/shard_map/ppermute | solution.py:23
  47.1 52.1 %collective-permute-start.1 = (bf16[24,1,128]{2,0,1:T(8,128)(2,1)}, bf16[24,1,128]{2,0,1:T(8,128)(2,1)}, u32[]{:S(2)}, u32[]{:S(2)}) collective-permute-start(bf16[24,1,128]{2,0,1:T(8,128)(2,1)} %get-tuple-element.190), channel_id=1, source_target_pairs={{0,2},{1,3},{2,0},{3,1},{4,6},{5,7},{6,4},{7,5},{8,10},{9,11},{10,... | collective-permute-start | bytes 18440 | tf_op jit(solution)/shard_map/ppermute | solution.py:23
  51.3 50.8 %collective-permute-start.2 = (bf16[24,1,128]{2,0,1:T(8,128)(2,1)}, bf16[24,1,128]{2,0,1:T(8,128)(2,1)}, u32[]{:S(2)}, u32[]{:S(2)}) collective-permute-start(bf16[24,1,128]{2,0,1:T(8,128)(2,1)} %get-tuple-element.189), channel_id=1, source_target_pairs={{0,3},{1,2},{2,1},{3,0},{4,7},{5,6},{6,5},{7,4},{8,11},{9,10},{10,... | collective-permute-start | bytes 18440 | tf_op jit(solution)/shard_map/ppermute | solution.py:23
  53.5 67.0 %collective-permute-start.3 = (bf16[24,1,128]{2,0,1:T(8,128)(2,1)}, bf16[24,1,128]{2,0,1:T(8,128)(2,1)}, u32[]{:S(2)}, u32[]{:S(2)}) collective-permute-start(bf16[24,1,128]{2,0,1:T(8,128)(2,1)} %get-tuple-element.188), channel_id=1, source_target_pairs={{0,4},{1,5},{2,6},{3,7},{4,0},{5,1},{6,2},{7,3},{8,12},{9,13},{10,... | collective-permute-start | bytes 18440 | tf_op jit(solution)/shard_map/ppermute | solution.py:23
  61.1 71.7 %collective-permute-start.4 = (bf16[24,1,128]{2,0,1:T(8,128)(2,1)}, bf16[24,1,128]{2,0,1:T(8,128)(2,1)}, u32[]{:S(2)}, u32[]{:S(2)}) collective-permute-start(bf16[24,1,128]{2,0,1:T(8,128)(2,1)} %get-tuple-element.187), channel_id=1, source_target_pairs={{0,5},{1,4},{2,7},{3,6},{4,1},{5,0},{6,3},{7,2},{8,13},{9,12},{10,... | collective-permute-start | bytes 18440 | tf_op jit(solution)/shard_map/ppermute | solution.py:23
  65.9 54.6 %copy-start.7 = (bf16[24,1,128]{2,0,1:T(8,128)(2,1)S(1)}, bf16[24,1,128]{2,0,1:T(8,128)(2,1)}, u32[]{:S(2)}) copy-start(bf16[24,1,128]{2,0,1:T(8,128)(2,1)} %get-tuple-element.183) | copy-start | bytes 18436
  65.9 119.0 %copy-start.3 = (bf16[384,256]{1,0:T(8,128)(2,1)S(1)}, bf16[384,256]{1,0:T(8,128)(2,1)}, u32[]{:S(2)}) copy-start(bf16[384,256]{1,0:T(8,128)(2,1)} %param.14) | copy-start | bytes 589828
  65.9 118.9 %copy-start.5 = (bf16[24,16,128]{2,0,1:T(8,128)(2,1)S(1)}, bf16[24,16,128]{2,0,1:T(8,128)(2,1)}, u32[]{:S(2)}) copy-start(bf16[24,16,128]{2,0,1:T(8,128)(2,1)} %copy-done.4) | copy-start | bytes 294916
  89.3 47.5 %collective-permute-start.5 = (bf16[24,1,128]{2,0,1:T(8,128)(2,1)}, bf16[24,1,128]{2,0,1:T(8,128)(2,1)S(1)}, u32[]{:S(2)}, u32[]{:S(2)}) collective-permute-start(bf16[24,1,128]{2,0,1:T(8,128)(2,1)} %get-tuple-element.186), channel_id=1, source_target_pairs={{0,6},{1,7},{2,4},{3,5},{4,2},{5,3},{6,0},{7,1},{8,14},{9,15},{10,... | collective-permute-start | bytes 18440 | tf_op jit(solution)/shard_map/ppermute | solution.py:23
  99.2 47.1 %collective-permute-start.6 = (bf16[24,1,128]{2,0,1:T(8,128)(2,1)}, bf16[24,1,128]{2,0,1:T(8,128)(2,1)S(1)}, u32[]{:S(2)}, u32[]{:S(2)}) collective-permute-start(bf16[24,1,128]{2,0,1:T(8,128)(2,1)} %get-tuple-element.185), channel_id=1, source_target_pairs={{0,7},{1,6},{2,5},{3,4},{4,3},{5,2},{6,1},{7,0},{8,15},{9,14},{10,... | collective-permute-start | bytes 18440 | tf_op jit(solution)/shard_map/ppermute | solution.py:23
  102.1 46.6 %collective-permute-start.7 = (bf16[24,1,128]{2,0,1:T(8,128)(2,1)}, bf16[24,1,128]{2,0,1:T(8,128)(2,1)}, u32[]{:S(2)}, u32[]{:S(2)}) collective-permute-start(bf16[24,1,128]{2,0,1:T(8,128)(2,1)} %get-tuple-element.184), channel_id=1, source_target_pairs={{0,8},{1,9},{2,10},{3,11},{4,12},{5,13},{6,14},{7,15},{8,0},{9,1},... | collective-permute-start | bytes 18440 | tf_op jit(solution)/shard_map/ppermute | solution.py:23
  114.7 1.4 copy-start.1
  116.1 70.7 %all-to-all-start.2 = ((bf16[256,16,128]{2,0,1:T(8,128)(2,1)}), bf16[256,16,128]{2,0,1:T(8,128)(2,1)S(1)}, u32[]{:S(2)}, u32[]{:S(2)}) async-start(bf16[256,16,128]{2,0,1:T(8,128)(2,1)} %bitcast.48), calls=%async_computation.2 | async-start | bytes 2097152 | tf_op jit(solution)/shard_map/all_to_all | solution.py:61
  119.7 234.5 %all-reduce.2.cloned.1.call-start = ((), (), s32[]{:S(2)}) async-start(), calls=%async_computation.4 | async-start | bytes 3932160 | tf_op jit(solution)/shard_map/psum | solution.py:115
  120.5 49.9 %collective-permute-start.8 = (bf16[24,1,128]{2,0,1:T(8,128)(2,1)S(1)}, bf16[24,1,128]{2,0,1:T(8,128)(2,1)S(1)}, u32[]{:S(2)}, u32[]{:S(2)}) collective-permute-start(bf16[24,1,128]{2,0,1:T(8,128)(2,1)S(1)} %copy-done.7), channel_id=1, source_target_pairs={{0,9},{1,8},{2,11},{3,10},{4,13},{5,12},{6,15},{7,14},{8,1},{9,0},... | collective-permute-start | bytes 18440 | tf_op jit(solution)/shard_map/ppermute | solution.py:23
  132.8 45.3 %collective-permute-start.9 = (bf16[24,1,128]{2,0,1:T(8,128)(2,1)S(1)}, bf16[24,1,128]{2,0,1:T(8,128)(2,1)S(1)}, u32[]{:S(2)}, u32[]{:S(2)}) collective-permute-start(bf16[24,1,128]{2,0,1:T(8,128)(2,1)S(1)} %get-tuple-element.182), channel_id=1, source_target_pairs={{0,10},{1,11},{2,8},{3,9},{4,14},{5,15},{6,12},{7,13},{8,2},{9,3},... | collective-permute-start | bytes 18440 | tf_op jit(solution)/shard_map/ppermute | solution.py:23
  136.8 45.9 %collective-permute-start.10 = (bf16[24,1,128]{2,0,1:T(8,128)(2,1)S(1)}, bf16[24,1,128]{2,0,1:T(8,128)(2,1)S(1)}, u32[]{:S(2)}, u32[]{:S(2)}) collective-permute-start(bf16[24,1,128]{2,0,1:T(8,128)(2,1)S(1)} %get-tuple-element.181), channel_id=1, source_target_pairs={{0,11},{1,10},{2,9},{3,8},{4,15},{5,14},{6,13},{7,12},{8,3},{9,2},... | collective-permute-start | bytes 18440 | tf_op jit(solution)/shard_map/ppermute | solution.py:23
  146.3 36.5 %collective-permute-start.11 = (bf16[24,1,128]{2,0,1:T(8,128)(2,1)S(1)}, bf16[24,1,128]{2,0,1:T(8,128)(2,1)S(1)}, u32[]{:S(2)}, u32[]{:S(2)}) collective-permute-start(bf16[24,1,128]{2,0,1:T(8,128)(2,1)S(1)} %get-tuple-element.180), channel_id=1, source_target_pairs={{0,12},{1,13},{2,14},{3,15},{4,8},{5,9},{6,10},{7,11},{8,4},{9,5},... | collective-permute-start | bytes 18440 | tf_op jit(solution)/shard_map/ppermute | solution.py:23
  148.7 34.1 %collective-permute-start.12 = (bf16[24,1,128]{2,0,1:T(8,128)(2,1)S(1)}, bf16[24,1,128]{2,0,1:T(8,128)(2,1)S(1)}, u32[]{:S(2)}, u32[]{:S(2)}) collective-permute-start(bf16[24,1,128]{2,0,1:T(8,128)(2,1)S(1)} %get-tuple-element.179), channel_id=1, source_target_pairs={{0,13},{1,12},{2,15},{3,14},{4,9},{5,8},{6,11},{7,10},{8,5},{9,4},... | collective-permute-start | bytes 18440 | tf_op jit(solution)/shard_map/ppermute | solution.py:23
  170.4 12.4 %collective-permute-start.13 = (bf16[24,1,128]{2,0,1:T(8,128)(2,1)S(1)}, bf16[24,1,128]{2,0,1:T(8,128)(2,1)S(1)}, u32[]{:S(2)}, u32[]{:S(2)}) collective-permute-start(bf16[24,1,128]{2,0,1:T(8,128)(2,1)S(1)} %get-tuple-element.178), channel_id=1, source_target_pairs={{0,14},{1,15},{2,12},{3,13},{4,10},{5,11},{6,8},{7,9},{8,6},{9,7},... | collective-permute-start | bytes 18440 | tf_op jit(solution)/shard_map/ppermute | solution.py:23
  178.1 6.7 %collective-permute-start.14 = (bf16[24,1,128]{2,0,1:T(8,128)(2,1)S(1)}, bf16[24,1,128]{2,0,1:T(8,128)(2,1)S(1)}, u32[]{:S(2)}, u32[]{:S(2)}) collective-permute-start(bf16[24,1,128]{2,0,1:T(8,128)(2,1)S(1)} %get-tuple-element.177), channel_id=1, source_target_pairs={{0,15},{1,14},{2,13},{3,12},{4,11},{5,10},{6,9},{7,8},{8,7},{9,6},... | collective-permute-start | bytes 18440 | tf_op jit(solution)/shard_map/ppermute | solution.py:23
  211.5 2.0 copy-start.8
  211.5 145.7 %all-gather.4.cloned.1.call-start = ((), (), s32[]{:S(2)}) async-start(), calls=%async_computation.5 | async-start | bytes 3379200 | tf_op jit(solution)/shard_map/all_gather | solution.py:123
  212.1 149.9 %all-gather.6.cloned.1.call-start = ((), (), s32[]{:S(2)}) async-start(), calls=%async_computation.6 | async-start | bytes 3379200 | tf_op jit(solution)/shard_map/all_gather | solution.py:128
  212.7 189.9 %all-gather.8.cloned.1.call-start = ((), (), s32[]{:S(2)}) async-start(), calls=%async_computation.7 | async-start | bytes 3379200 | tf_op jit(solution)/shard_map/all_gather | solution.py:134
  213.3 270.5 %reduce-scatter.2.cloned.1.call-start = ((), (), s32[]{:S(2)}) async-start(), calls=%async_computation.8 | async-start | bytes 2088960 | tf_op jit(solution)/shard_map/reduce_scatter | solution.py:138
Sparse Core Ops, SparseCore 0:
  211.7 142.5 all-reduce.1
  410.9 72.8 reduce-scatter.1
Sparse Core Ops, SparseCore 1:
  215.7 59.6 all-gather.3
  278.9 59.9 all-gather.5
  342.4 60.1 all-gather.7
